TPU v7x, 256 devices: a whole 4x4x8 slice. The times are simulated.
256 devices in a mesh: chan: 64 (over x, y, z_hi, core), beam: 4 (over z_lo).
Axes of the slice: x: 4, y: 4, z: 8 (z_hi: 2, z_lo: 4; z = z_hi * 4 + z_lo), core: 2. Of those that a mesh axis runs over, the one named last changes fastest.
Arguments:
- images: float32 [256, 36, 128, 128], P('chan', 'beam')
- beam_weight: float32 [36, 128, 128], P('beam'), may hold values from 0.2 to 1
- offsets: int32 [36, 2], P('beam'), may hold values from 0 to 384, as said below
- rejected_indicator: int32 [256, 192, 512], P('chan', None, 'beam'), may hold values 0 or 1
- regression_indicator: int32 [256], replicated, may hold values 0 or 1
Outputs:
- cleaned_cube: float32 [256, 192, 512], P(None, 'chan', 'beam')
Inputs may be any that keep to these rules, and one draw needn't show every extreme that they name: `offsets`: beam b = 6 r + q sits near row r * 64 // 5 and column q * 384 // 5, within 16; every sky pixel is covered by some beam; the first and last row and column of beams lie at the field's edges.
All inputs are finite; a program needn't handle non-finite values. No bound on the sum of `rejected_indicator` on one device may be relied on, other than what follows from the above.
Results may differ from a plain program's by a relative error of at most 0.00023.
Values sent between devices are 32-bit elements; how exact they have to be, the bound alone decides.
No kernel may reach another device: no remote copies, remote signals or barrier semaphores. Data moves between devices by JAX's collectives and lax.ppermute only.
A program may use at most 128 MiB of HBM per device.

v0:
```python
import jax
import jax.numpy as jnp
from jax import lax
from jax.sharding import PartitionSpec as P

MOS_ROWS = 192
MOS_COLS = 512


def legendre(count):
    position = (2.0 * jnp.arange(count).astype(jnp.float32) + 1.0) / count - 1.0
    square = position * position
    return jnp.stack(
        [
            jnp.ones_like(position),
            position,
            0.5 * (3.0 * square - 1.0),
            0.5 * (5.0 * square * position - 3.0 * position),
        ],
        axis=1,
    )


def solve_cubic(normal_matrix, right_side):
    factor = {}
    for outer in range(4):
        for inner in range(outer + 1):
            value = normal_matrix[outer * 4 + inner]
            for other in range(inner):
                value = value - factor[outer, other] * factor[inner, other]
            if outer == inner:
                factor[outer, outer] = jnp.sqrt(value)
            else:
                factor[outer, inner] = value / factor[inner, inner]
    forward = []
    for outer in range(4):
        value = right_side[outer]
        for other in range(outer):
            value = value - factor[outer, other] * forward[other]
        forward.append(value / factor[outer, outer])
    backward = [None] * 4
    for outer in range(3, -1, -1):
        value = forward[outer]
        for other in range(outer + 1, 4):
            value = value - factor[other, outer] * backward[other]
        backward[outer] = value / factor[outer, outer]
    return jnp.stack(backward, axis=0)


def clean_pair(pair):
    sky_tile, weight_tile = pair
    channels, rows, columns = sky_tile.shape
    celestial_image = sky_tile.reshape(channels, rows * columns)
    importance_factor = weight_tile.reshape(channels, rows * columns)
    table = legendre(channels)
    products = jnp.stack(
        [table[:, outer] * table[:, inner] for outer in range(4) for inner in range(4)], axis=0
    )
    normal_matrix = jnp.dot(
        products,
        importance_factor,
        precision=lax.Precision.HIGHEST,
        preferred_element_type=jnp.float32,
    )
    right_side = jnp.dot(
        table.T,
        importance_factor * celestial_image,
        precision=lax.Precision.HIGHEST,
        preferred_element_type=jnp.float32,
    )
    coefficients = solve_cubic(normal_matrix, right_side)
    continuum = jnp.dot(
        table, coefficients, precision=lax.Precision.HIGHEST, preferred_element_type=jnp.float32
    )
    residual = celestial_image - continuum
    padded = jnp.pad(residual, ((1, 1), (0, 0)))
    smoothed = 0.25 * padded[:-2] + 0.5 * residual + 0.25 * padded[2:]
    return smoothed.reshape(channels, rows, columns)


def place(values, row_start, col_start, side, columns, first_column):
    row_hit = (
        lax.broadcasted_iota(jnp.int32, (1, MOS_ROWS, side), 1)
        == lax.broadcasted_iota(jnp.int32, (1, MOS_ROWS, side), 2) + row_start[:, None, None]
    ).astype(jnp.float32)
    col_hit = (
        lax.broadcasted_iota(jnp.int32, (1, side, columns), 2) + first_column
        == lax.broadcasted_iota(jnp.int32, (1, side, columns), 1) + col_start[:, None, None]
    ).astype(jnp.float32)
    rows_placed = jnp.einsum(
        "bri,cbij->bcrj",
        row_hit,
        values,
        precision=lax.Precision.HIGHEST,
        preferred_element_type=jnp.float32,
    )
    return jnp.einsum(
        "bcrj,bjk->crk",
        rows_placed,
        col_hit,
        precision=lax.Precision.HIGHEST,
        preferred_element_type=jnp.float32,
    )


def local(images, beam_weight, offsets, rejected_indicator, regression_indicator):
    ch_dev = images.shape[0]
    side = images.shape[2]
    col_dev = rejected_indicator.shape[2]
    all_channels = regression_indicator.shape[0]
    first_channel = lax.axis_index("chan") * ch_dev
    channel_ids = first_channel + jnp.arange(ch_dev, dtype=jnp.int32)
    exponent = 1.0 + 0.5 * channel_ids.astype(jnp.float32) / (all_channels - 1)
    row_start = jnp.clip(offsets[:, 0], 0, MOS_ROWS - side)
    col_start = jnp.clip(offsets[:, 1], 0, MOS_COLS - side)
    log_weight = jnp.log(beam_weight)
    core = lax.axis_index("chan") % 2
    half = side // 2
    own_half = lax.dynamic_slice_in_dim(log_weight, core * half, half, 1)
    corner = jnp.zeros((log_weight.shape[0], 8, side), jnp.float32)
    corner = corner.at[:, 0, 0].set(row_start.astype(jnp.float32))
    corner = corner.at[:, 0, 1].set(col_start.astype(jnp.float32))
    shared = lax.all_gather(jnp.concatenate([own_half, corner], axis=1), "beam", axis=0, tiled=True)
    chan_size = lax.psum(1, "chan")
    other = lax.ppermute(shared, "chan", [(a, a ^ 1) for a in range(chan_size)])
    first_half = jnp.where(core == 0, shared, other)
    second_half = jnp.where(core == 0, other, shared)
    every_log = jnp.concatenate([first_half[:, :half], second_half[:, :half]], axis=1)
    every_row = first_half[:, half, 0].astype(jnp.int32)
    every_col = first_half[:, half, 1].astype(jnp.int32)
    response = jnp.exp(exponent[:, None, None, None] * log_weight[None])
    numerator = place(response * images, row_start, col_start, side, MOS_COLS, 0)
    dividend_accumulator = lax.psum_scatter(numerator, "beam", scatter_dimension=2, tiled=True)
    every_response = jnp.exp(exponent[:, None, None, None] * every_log[None])
    col_first = lax.axis_index("beam") * col_dev
    normalizer_accumulated = place(
        every_response * every_response, every_row, every_col, side, col_dev, col_first
    )
    accepted_entries = 1.0 - rejected_indicator.astype(jnp.float32)
    emission_absent = lax.dynamic_slice_in_dim(regression_indicator, first_channel, ch_dev).astype(
        jnp.float32
    )
    celestial_image = accepted_entries * dividend_accumulator / normalizer_accumulated
    importance_factor = normalizer_accumulated * (
        emission_absent[:, None, None] * accepted_entries + 0.01
    )
    arrived = lax.all_to_all(
        jnp.stack([celestial_image, importance_factor]),
        "chan",
        split_axis=2,
        concat_axis=1,
        tiled=True,
    )
    return clean_pair((arrived[0], arrived[1]))


def solution(mesh):
    in_specs = (
        P("chan", "beam", None, None),
        P("beam", None, None),
        P("beam", None),
        P("chan", None, "beam"),
        P(),
    )
    out_specs = P(None, "chan", "beam")
    return jax.shard_map(local, mesh=mesh, in_specs=in_specs, out_specs=out_specs, check_vma=False)
```

profile of v0, /device:TPU:33, one launch (start us, length us, event | category | flops | bytes accessed | tf_op | source)
XLA Modules:
  0.0 153.1 jit_solution(11954396857030517619)
XLA Ops:
  6.5 1.3 log.3
  7.8 0.8 fusion.76
  8.6 0.6 fusion.83
  9.2 1.2 scatter.9
  10.5 0.2 copy.16
  10.7 0.8 pad_maximum_fusion.2
  11.5 2.3 %fusion.12 = f32[9,4,128,192]{2,3,0,1:T(8,128)S(1)} fusion(f32[4,9,128,128]{3,2,1,0:T(8,128)S(1)} %copy-done.1, f32[9,128,128]{2,1,0:T(8,128)S(1)} %log.3, f32[4]{0:T(128)S(1)} %multiply_add_fusion.3, s32[9]{0:T(128)S(1)} %get-tuple-element.51), kind=kOutput, calls=%fused_computation.15 | convolution fusion | flops 1360576512 | bytes 6488116 | tf_op jit(solution)/shard_map/bri,cbij->bcrj/dot_general | solution.py:90
  13.9 4.6 %fusion.21 = f32[4,192,512]{2,1,0:T(8,128)} fusion(f32[9,4,128,192]{2,3,0,1:T(8,128)S(1)} %fusion.12, s32[9]{0:T(128)S(1)} %get-tuple-element.48), kind=kOutput, calls=%fused_computation.22 | convolution fusion | flops 5436997632 | bytes 5111844 | tf_op jit(solution)/shard_map/bcrj,bjk->crk/dot_general | solution.py:97
  18.5 31.4 %all-gather.2.cloned.1.call-done = f32[36,72,128]{2,1,0:T(8,128)} async-done(((f32[9,72,128]{2,1,0:T(8,128)}), f32[36,72,128]{2,1,0:T(8,128)}) %all-gather.2.cloned.1.call-update) | async-done | bytes 1327120 | tf_op jit(solution)/shard_map/all_gather | solution.py:123
  49.9 1.4 collective-permute-start
  51.4 2.8 %collective-permute-done = f32[36,72,128]{2,1,0:T(8,128)S(1)} collective-permute-done((f32[36,72,128]{2,1,0:T(8,128)}, f32[36,72,128]{2,1,0:T(8,128)S(1)}, u32[]{:S(2)}, u32[]{:S(2)}) %collective-permute-start) | collective-permute-done | bytes 1327136 | tf_op jit(solution)/shard_map/ppermute | solution.py:125
  54.2 0.1 broadcast_select_fusion
  54.3 0.1 slice.145
  54.5 1.4 fusion.46
  55.9 0.2 slice_select_fusion
  56.1 0.2 pad_maximum_fusion
  56.3 11.5 %fusion.2 = f32[36,4,128,192]{2,3,0,1:T(8,128)} fusion(f32[36,128,128]{2,1,0:T(8,128)S(1)} %pad_maximum_fusion, f32[4]{0:T(128)S(1)} %multiply_add_fusion.3, s32[36]{0:T(128)S(1)} %get-tuple-element.30), kind=kOutput, calls=%fused_computation.2 | convolution fusion | flops 5442306048 | bytes 16515232 | tf_op jit(solution)/shard_map/bri,cbij->bcrj/dot_general | solution.py:90
  67.7 24.5 %reduce-scatter.2.cloned.1.call-done = f32[4,192,128]{2,1,0:T(8,128)} async-done(((f32[4,192,512]{2,1,0:T(8,128)}), f32[4,192,128]{2,1,0:T(8,128)}) %reduce-scatter.2.cloned.1.call-update) | async-done | bytes 393232 | tf_op jit(solution)/shard_map/reduce_scatter | solution.py:133
  92.2 10.1 %divide_bitcast_fusion = (f32[1,4,192,128]{3,2,1,0:T(8,128)S(1)}, f32[1,4,192,128]{3,2,1,0:T(8,128)S(1)}) fusion(f32[4,192,128]{2,1,0:T(8,128)} %reduce-scatter.2.cloned.1.call-done, s32[4,192,128]{2,1,0:T(8,128)S(1)} %copy-done.2, f32[4]{0:T(128)S(1)} %dynamic-slice_convert_fusion, s32[36]{0:T(128)S(1)} %get-tuple-element.29, s32[128]{0:T(128)S(1)} %iota_add_fusion, ...), kind=kOutput, calls=%fused_computation.43 | convolution fusion | flops 5437685760 | bytes 15729312 | tf_op jit(solution)/shard_map/bcrj,bjk->crk/dot_general | solution.py:97
  102.4 1.4 copy.17
  103.9 12.4 %all-to-all-start = ((f32[2,4,192,128]{3,1,0,2:T(4,128)}), f32[2,4,192,128]{3,1,0,2:T(4,128)S(1)}, u32[]{:S(2)}, u32[]{:S(2)}) async-start(f32[2,4,192,128]{3,1,0,2:T(4,128)} %copy.17), calls=%async_computation.1 | async-start | bytes 1572864 | tf_op jit(solution)/shard_map/all_to_all | solution.py:147
  116.4 26.7 %all-to-all-done = f32[2,4,192,128]{3,1,0,2:T(4,128)S(1)} async-done(((f32[2,4,192,128]{3,1,0,2:T(4,128)}), f32[2,4,192,128]{3,1,0,2:T(4,128)S(1)}, u32[]{:S(2)}, u32[]{:S(2)}) %all-to-all-start) | async-done | bytes 786464 | tf_op jit(solution)/shard_map/all_to_all | solution.py:147
  143.1 0.1 copy.18
  143.4 0.1 copy.19
  143.5 0.1 copy.20
  143.6 0.3 fusion.39
  143.9 0.3 fusion.41
  144.2 0.1 fusion.64
  144.4 0.7 convolution_subtract_fusion
  145.1 0.1 multiply_add_fusion
  145.2 0.2 copy.21
  145.4 0.9 copy.22
  (32 shorter events, 0.6 us)
Async XLA Ops:
  6.5 5.0 %copy-start.1 = (f32[4,9,128,128]{3,2,1,0:T(8,128)S(1)}, f32[4,9,128,128]{3,2,1,0:T(8,128)}, u32[]{:S(2)}) copy-start(f32[4,9,128,128]{3,2,1,0:T(8,128)} %param.9) | copy-start | bytes 7077892
  6.5 43.3 %all-gather.2.cloned.1.call-start = ((), (), s32[]{:S(2)}) async-start(), calls=%async_computation.3 | async-start | bytes 1658880 | tf_op jit(solution)/shard_map/all_gather | solution.py:123
  11.5 80.8 %reduce-scatter.2.cloned.1.call-start = ((), (), s32[]{:S(2)}) async-start(), calls=%async_computation.2 | async-start | bytes 1966080 | tf_op jit(solution)/shard_map/reduce_scatter | solution.py:133
  13.9 37.4 %copy-start.3 = (s32[256]{0:T(256)S(1)}, s32[256]{0:T(256)}, u32[]{:S(2)}) copy-start(s32[256]{0:T(256)} %param.13) | copy-start | bytes 3076
  49.9 4.3 %collective-permute-start = (f32[36,72,128]{2,1,0:T(8,128)}, f32[36,72,128]{2,1,0:T(8,128)S(1)}, u32[]{:S(2)}, u32[]{:S(2)}) collective-permute-start(f32[36,72,128]{2,1,0:T(8,128)} %all-gather.2.cloned.1.call-done), channel_id=1, source_target_pairs={{0,4},{4,0},{8,12},{12,8},{16,20},{20,16},{24,28},{28,24},{32,36},... | collective-permute-start | bytes 3981320 | tf_op jit(solution)/shard_map/ppermute | solution.py:125
  51.4 4.5 %copy-start = (f32[36,72,128]{2,1,0:T(8,128)S(1)}, f32[36,72,128]{2,1,0:T(8,128)}, u32[]{:S(2)}) copy-start(f32[36,72,128]{2,1,0:T(8,128)} %all-gather.2.cloned.1.call-done) | copy-start | bytes 3981316
  56.3 36.0 %copy-start.2 = (s32[4,192,128]{2,1,0:T(8,128)S(1)}, s32[4,192,128]{2,1,0:T(8,128)}, u32[]{:S(2)}) copy-start(s32[4,192,128]{2,1,0:T(8,128)} %param.12) | copy-start | bytes 1179652
  103.9 39.3 %all-to-all-start = ((f32[2,4,192,128]{3,1,0,2:T(4,128)}), f32[2,4,192,128]{3,1,0,2:T(4,128)S(1)}, u32[]{:S(2)}, u32[]{:S(2)}) async-start(f32[2,4,192,128]{3,1,0,2:T(4,128)} %copy.17), calls=%async_computation.1 | async-start | bytes 1572864 | tf_op jit(solution)/shard_map/all_to_all | solution.py:147
Sparse Core Ops, SparseCore 0:
  11.6 38.2 all-gather.1
  52.4 39.7 reduce-scatter.1
where the time goes:
time: 153 us
  waiting for transfers between devices  85.5 us (56%)
  matrix products  29.8 us (19%)
  starting transfers between devices  13.8 us (9%)
  between operations  13.6 us (9%)
  local copies, waits for them, and re-layouts  6.56 us (4%)
  other arithmetic  3.96 us (3%)
    all_gather x1, waiting for transfers between devices, local(): lax.all_gather(jnp.concatenate([own_half, corner], axis=1), 'beam', axis=...  31.4 us
    all_to_all x1, waiting for transfers between devices, local(): lax.all_to_all(jnp.stack([celestial_image, importance_factor]), 'chan', s...  26.7 us
    reduce_scatter x1, waiting for transfers between devices, local(): lax.psum_scatter(numerator, 'beam', scatter_dimension=2, tiled=True)  24.5 us
    dot_general x2, matrix products, place(): jnp.einsum('bcrj,bjk->crk', rows_placed, col_hit, precision=lax.Precision...  14.8 us
    dot_general x2, matrix products, place(): jnp.einsum('bri,cbij->bcrj', row_hit, values, precision=lax.Precision.HIG...  13.8 us
    all_to_all x1, starting transfers between devices, local(): lax.all_to_all(jnp.stack([celestial_image, importance_factor]), 'chan', s...  12.4 us
  transfers between devices with their start and end apart: 4, of which 4 were waited for; matrix products, arithmetic and copies ran while one was open for 14% of the time, Pallas kernels for 0%

commit v1 on v0

--- a/solution.py
+++ b/solution.py
@@ -5,6 +5,15 @@
 
 MOS_ROWS = 192
 MOS_COLS = 512
+cut_the_rows = lambda xx: jnp.concatenate(
+    lax.all_to_all(
+        jnp.stack([xx for _ in range(lax.axis_size("beam"))]),
+        axis_name="beam",
+        split_axis=0,
+        concat_axis=0,
+    ),
+    axis=0,
+)
 
 
 def legendre(count):
@@ -120,7 +129,7 @@
     corner = jnp.zeros((log_weight.shape[0], 8, side), jnp.float32)
     corner = corner.at[:, 0, 0].set(row_start.astype(jnp.float32))
     corner = corner.at[:, 0, 1].set(col_start.astype(jnp.float32))
-    shared = lax.all_gather(jnp.concatenate([own_half, corner], axis=1), "beam", axis=0, tiled=True)
+    shared = cut_the_rows(jnp.concatenate([own_half, corner], axis=1))
     chan_size = lax.psum(1, "chan")
     other = lax.ppermute(shared, "chan", [(a, a ^ 1) for a in range(chan_size)])
     first_half = jnp.where(core == 0, shared, other)

time: 153 us -> 146 us (0.954)
  the two profiles are of different devices: /device:TPU:33 before, /device:TPU:1 now
where the time goes in v1:
time: 146 us
  waiting for transfers between devices  64 us (44%)
  matrix products  31.5 us (22%)
  starting transfers between devices  25.8 us (18%)
  between operations  13.6 us (9%)
  local copies, waits for them, and re-layouts  7.66 us (5%)
  other arithmetic  3.23 us (2%)
    all_to_all x1, waiting for transfers between devices, lax.all_to_all(jnp.stack([xx for _ in range(lax.axis_size('beam'))]), axi...  36.8 us
    all_to_all x1, waiting for transfers between devices, local(): lax.all_to_all(jnp.stack([celestial_image, importance_factor]), 'chan', s...  24.6 us
    dot_general x2, matrix products, place(): jnp.einsum('bri,cbij->bcrj', row_hit, values, precision=lax.Precision.HIG...  15.5 us
    dot_general x2, matrix products, place(): jnp.einsum('bcrj,bjk->crk', rows_placed, col_hit, precision=lax.Precision...  14.8 us
    all_to_all x1, starting transfers between devices, local(): lax.all_to_all(jnp.stack([celestial_image, importance_factor]), 'chan', s...  14 us
    all_to_all x1, starting transfers between devices, lax.all_to_all(jnp.stack([xx for _ in range(lax.axis_size('beam'))]), axi...  6.43 us
    ppermute x1, starting transfers between devices, local(): other = lax.ppermute(shared, 'chan', [(a, a ^ 1) for a in range(chan_size)])  5.38 us
  transfers between devices with their start and end apart: 4, of which 3 were waited for; matrix products, arithmetic and copies ran while one was open for 15% of the time, Pallas kernels for 0%

profile of v1, /device:TPU:1, one launch (start us, length us, event | category | flops | bytes accessed | tf_op | source)
XLA Modules:
  0.0 145.7 jit_solution(12271616327910466324)
XLA Ops:
  6.5 1.1 log.3
  7.7 0.8 fusion.76
  8.5 0.6 fusion.83
  9.1 1.3 scatter.9
  10.4 0.2 copy.24
  10.7 1.2 stack.14
  11.8 6.4 %all-to-all-start = ((f32[4,9,72,128]{3,2,1,0:T(8,128)}), f32[4,9,72,128]{3,2,1,0:T(8,128)S(1)}, u32[]{:S(2)}, u32[]{:S(2)}) async-start(f32[4,9,72,128]{3,2,1,0:T(8,128)} %stack.14), calls=%async_computation.1 | async-start | bytes 2654208 | tf_op jit(solution)/shard_map/all_to_all | solution.py:9
  18.3 4.0 %fusion.12 = f32[9,4,128,192]{2,3,0,1:T(8,128)S(1)} fusion(f32[4,9,128,128]{3,2,1,0:T(8,128)} %param.9, f32[9,128,128]{2,1,0:T(8,128)S(1)} %log.3, f32[4]{0:T(128)S(1)} %multiply_add_fusion.3, s32[9]{0:T(128)S(1)} %get-tuple-element.51), kind=kOutput, calls=%fused_computation.15 | convolution fusion | flops 1360576512 | bytes 6488116 | tf_op jit(solution)/shard_map/bri,cbij->bcrj/dot_general | solution.py:99
  22.3 4.6 %fusion.21 = f32[4,192,512]{2,1,0:T(8,128)} fusion(f32[9,4,128,192]{2,3,0,1:T(8,128)S(1)} %fusion.12, s32[9]{0:T(128)S(1)} %get-tuple-element.48), kind=kOutput, calls=%fused_computation.22 | convolution fusion | flops 5436997632 | bytes 5111844 | tf_op jit(solution)/shard_map/bcrj,bjk->crk/dot_general | solution.py:106
  26.9 36.8 %all-to-all-done = f32[4,9,72,128]{3,2,1,0:T(8,128)S(1)} async-done(((f32[4,9,72,128]{3,2,1,0:T(8,128)}), f32[4,9,72,128]{3,2,1,0:T(8,128)S(1)}, u32[]{:S(2)}, u32[]{:S(2)}) %all-to-all-start) | async-done | bytes 1327136 | tf_op jit(solution)/shard_map/all_to_all | solution.py:9
  63.6 5.4 %collective-permute-start = (f32[36,72,128]{2,1,0:T(8,128)S(1)}, f32[36,72,128]{2,1,0:T(8,128)S(1)}, u32[]{:S(2)}, u32[]{:S(2)}) collective-permute-start(f32[36,72,128]{2,1,0:T(8,128)S(1)} %bitcast.74), channel_id=1, source_target_pairs={{0,4},{4,0},{8,12},{12,8},{16,20},{20,16},{24,28},{28,24},{32,36},... | collective-permute-start | bytes 3981320 | tf_op jit(solution)/shard_map/ppermute | solution.py:134
  69.1 2.6 %collective-permute-done = f32[36,72,128]{2,1,0:T(8,128)S(1)} collective-permute-done((f32[36,72,128]{2,1,0:T(8,128)S(1)}, f32[36,72,128]{2,1,0:T(8,128)S(1)}, u32[]{:S(2)}, u32[]{:S(2)}) %collective-permute-start) | collective-permute-done | bytes 1327136 | tf_op jit(solution)/shard_map/ppermute | solution.py:134
  71.7 0.1 broadcast_select_fusion
  71.8 0.1 slice.145
  72.0 1.4 fusion.46
  73.4 0.2 slice_select_fusion
  73.6 0.2 pad_maximum_fusion
  73.8 11.5 %fusion.2 = f32[36,4,128,192]{2,3,0,1:T(8,128)} fusion(f32[36,128,128]{2,1,0:T(8,128)S(1)} %pad_maximum_fusion, f32[4]{0:T(128)S(1)} %multiply_add_fusion.3, s32[36]{0:T(128)S(1)} %get-tuple-element.30), kind=kOutput, calls=%fused_computation.2 | convolution fusion | flops 5442306048 | bytes 16515232 | tf_op jit(solution)/shard_map/bri,cbij->bcrj/dot_general | solution.py:99
  85.3 10.2 %divide_bitcast_fusion = (f32[1,4,192,128]{3,2,1,0:T(8,128)S(1)}, f32[1,4,192,128]{3,2,1,0:T(8,128)S(1)}) fusion(f32[4,192,128]{2,1,0:T(8,128)} %reduce-scatter.2.cloned.1.call-done, s32[4,192,128]{2,1,0:T(8,128)S(1)} %copy-done, f32[4]{0:T(128)S(1)} %dynamic-slice_convert_fusion, s32[36]{0:T(128)S(1)} %get-tuple-element.29, s32[128]{0:T(128)S(1)} %iota_add_fusion, ...), kind=kOutput, calls=%fused_computation.43 | convolution fusion | flops 5437685760 | bytes 15729312 | tf_op jit(solution)/shard_map/bcrj,bjk->crk/dot_general | solution.py:106
  95.5 1.4 copy.25
  96.9 14.0 %all-to-all-start.1 = ((f32[2,4,192,128]{3,1,0,2:T(4,128)}), f32[2,4,192,128]{3,1,0,2:T(4,128)S(1)}, u32[]{:S(2)}, u32[]{:S(2)}) async-start(f32[2,4,192,128]{3,1,0,2:T(4,128)} %copy.25), calls=%async_computation.2 | async-start | bytes 1572864 | tf_op jit(solution)/shard_map/all_to_all | solution.py:156
  111.1 24.6 %all-to-all-done.1 = f32[2,4,192,128]{3,1,0,2:T(4,128)S(1)} async-done(((f32[2,4,192,128]{3,1,0,2:T(4,128)}), f32[2,4,192,128]{3,1,0,2:T(4,128)S(1)}, u32[]{:S(2)}, u32[]{:S(2)}) %all-to-all-start.1) | async-done | bytes 786464 | tf_op jit(solution)/shard_map/all_to_all | solution.py:156
  135.7 0.1 copy.26
  135.9 0.1 copy.27
  136.1 0.1 copy.28
  136.2 0.3 fusion.39
  136.5 0.3 fusion.41
  136.8 0.1 fusion.64
  137.0 0.7 convolution_subtract_fusion
  137.7 0.1 multiply_add_fusion
  137.8 0.2 copy.29
  138.0 0.9 copy.30
  (28 shorter events, 0.6 us)
Async XLA Ops:
  11.8 51.8 %all-to-all-start = ((f32[4,9,72,128]{3,2,1,0:T(8,128)}), f32[4,9,72,128]{3,2,1,0:T(8,128)S(1)}, u32[]{:S(2)}, u32[]{:S(2)}) async-start(f32[4,9,72,128]{3,2,1,0:T(8,128)} %stack.14), calls=%async_computation.1 | async-start | bytes 2654208 | tf_op jit(solution)/shard_map/all_to_all | solution.py:9
  18.2 67.0 %reduce-scatter.2.cloned.1.call-start = ((), (), s32[]{:S(2)}) async-start(), calls=%async_computation.3 | async-start | bytes 1966080 | tf_op jit(solution)/shard_map/reduce_scatter | solution.py:142
  22.2 46.8 %copy-start.1 = (s32[256]{0:T(256)S(1)}, s32[256]{0:T(256)}, u32[]{:S(2)}) copy-start(s32[256]{0:T(256)} %param.13) | copy-start | bytes 3076
  63.6 8.1 %collective-permute-start = (f32[36,72,128]{2,1,0:T(8,128)S(1)}, f32[36,72,128]{2,1,0:T(8,128)S(1)}, u32[]{:S(2)}, u32[]{:S(2)}) collective-permute-start(f32[36,72,128]{2,1,0:T(8,128)S(1)} %bitcast.74), channel_id=1, source_target_pairs={{0,4},{4,0},{8,12},{12,8},{16,20},{20,16},{24,28},{28,24},{32,36},... | collective-permute-start | bytes 3981320 | tf_op jit(solution)/shard_map/ppermute | solution.py:134
  73.8 11.5 %copy-start = (s32[4,192,128]{2,1,0:T(8,128)S(1)}, s32[4,192,128]{2,1,0:T(8,128)}, u32[]{:S(2)}) copy-start(s32[4,192,128]{2,1,0:T(8,128)} %param.12) | copy-start | bytes 1179652
  96.9 38.8 %all-to-all-start.1 = ((f32[2,4,192,128]{3,1,0,2:T(4,128)}), f32[2,4,192,128]{3,1,0,2:T(4,128)S(1)}, u32[]{:S(2)}, u32[]{:S(2)}) async-start(f32[2,4,192,128]{3,1,0,2:T(4,128)} %copy.25), calls=%async_computation.2 | async-start | bytes 1572864 | tf_op jit(solution)/shard_map/all_to_all | solution.py:156
Sparse Core Ops, SparseCore 0:
  27.0 47.5 reduce-scatter.1
